TPU v7x, 32 devices: a whole 2x2x4 slice. The times are simulated.
32 devices in a mesh: groups: 2 (over y), frames: 4 (over z), heads: 4 (over x, core).
Axes of the slice: x: 2, y: 2, z: 4, core: 2. Of those that a mesh axis runs over, the one named last changes fastest.
Arguments:
- query_heads: bfloat16 [16384, 896], P(('groups', 'frames'), 'heads'), parts along dimension 0, may hold values from -6 to 6
- key_heads: bfloat16 [16384, 896], P(('groups', 'frames'), 'heads'), parts along dimension 0, may hold values from -0.04 to 8
- value_heads: bfloat16 [16384, 896], P(('groups', 'frames'), 'heads'), parts along dimension 0, may hold values from -6 to 6
- residual: bfloat16 [16384, 2240], P(('groups', 'frames', 'heads')), parts along dimension 0, may hold values from -6 to 6
- out_proj: bfloat16 [896, 2240], P('frames'), may hold values from -0.1875 to 0.1875
- frame_gate: float32 [32, 2240], P(('groups', 'frames')), parts along dimension 0, may hold values from -4 to 4
Outputs:
- updated: bfloat16 [16384, 2240], P(('groups', 'frames', 'heads')), parts along dimension 0
There are 2 independent parts, one for each index of `groups`. A program takes and returns all parts, laid end to end along the dimension named above; an argument that names none is the same for every part. Nothing has to cross between parts.
All inputs are finite; a program needn't handle non-finite values.
Results may differ from a plain program's by a relative error of at most 0.0033.
Values may be sent and summed in bfloat16 or wider, within the bound.
No kernel may reach another device: no remote copies, remote signals or barrier semaphores. Data moves between devices by JAX's collectives and lax.ppermute only.
A program may use at most 64 MiB of HBM per device.

v0:
```python
import jax
import jax.numpy as jnp
from jax import lax
from jax.sharding import PartitionSpec as P

HD = 112
HEADS_DEV = 2
FRAME_TOK = 512


EPSILON = 1e-06


def per_device(query_heads, key_heads, value_heads, residual, out_proj, frame_gate):
    length = query_heads.shape[0]
    frames_here = length // FRAME_TOK
    block_shape = (frames_here, FRAME_TOK, HEADS_DEV, HD)
    query_pos = jnp.maximum(query_heads, 0).reshape(block_shape)
    key_pos = jnp.maximum(key_heads, 0).reshape(block_shape)
    value_frames = value_heads.reshape(block_shape)
    frame_state = jnp.einsum(
        "fthi,fthj->fhij", key_pos, value_frames, preferred_element_type=jnp.float32
    )
    frame_sum = jnp.sum(key_pos, axis=1, dtype=jnp.float32)
    own_state = jnp.sum(frame_state, axis=0)
    own_sum = jnp.sum(frame_sum, axis=0)
    position = lax.axis_index("frames")
    gathered = (
        lax.all_gather(own_state[None], "frames", axis=0, tiled=True),
        lax.all_gather(own_sum[None], "frames", axis=0, tiled=True),
    )
    pieces = gathered[0].shape[0]
    is_lower = jnp.arange(pieces, dtype=jnp.int32) < position
    state_part = jnp.sum(jnp.where(is_lower[:, None, None, None], gathered[0], 0.0), axis=0)
    sum_part = jnp.sum(jnp.where(is_lower[:, None, None], gathered[1], 0.0), axis=0)
    prefix_state = state_part[None] + jnp.cumsum(frame_state, axis=0)
    prefix_sum = sum_part[None] + jnp.cumsum(frame_sum, axis=0)
    state_round = prefix_state.astype(jnp.bfloat16)
    sum_round = prefix_sum.astype(jnp.bfloat16)
    numerator = jnp.einsum(
        "fthi,fhij->fthj", query_pos, state_round, preferred_element_type=jnp.float32
    )
    denominator = (
        jnp.einsum("fthi,fhi->fth", query_pos, sum_round, preferred_element_type=jnp.float32)
        + EPSILON
    )
    attended = (
        (numerator / denominator[..., None]).astype(jnp.bfloat16).reshape(length, HEADS_DEV * HD)
    )
    rows_here = residual.shape[0]
    head_pos = lax.axis_index("heads")
    row_frame = (head_pos * rows_here + jnp.arange(rows_here, dtype=jnp.int32)) // FRAME_TOK
    selector = (row_frame[:, None] == jnp.arange(frames_here, dtype=jnp.int32)[None, :]).astype(
        jnp.float32
    )
    gate_rows = jnp.dot(
        selector, frame_gate, precision=lax.Precision.HIGHEST, preferred_element_type=jnp.float32
    )
    token_rows = lax.all_to_all(attended, "heads", split_axis=0, concat_axis=1, tiled=True)
    projected = jnp.dot(
        token_rows,
        lax.all_gather(out_proj, "frames", axis=0, tiled=True),
        preferred_element_type=jnp.float32,
    )
    return (residual.astype(jnp.float32) + gate_rows * projected).astype(jnp.bfloat16)


def solution(mesh):
    in_specs = (
        P(("groups", "frames"), "heads"),
        P(("groups", "frames"), "heads"),
        P(("groups", "frames"), "heads"),
        P(("groups", "frames", "heads"), None),
        P("frames", None),
        P(("groups", "frames"), None),
    )
    out_specs = P(("groups", "frames", "heads"), None)
    return jax.shard_map(
        per_device, mesh=mesh, in_specs=in_specs, out_specs=out_specs, check_vma=False
    )
```

profile of v0, /device:TPU:0, one launch (start us, length us, event | category | flops | bytes accessed | tf_op | source)
XLA Modules:
  0.0 113.2 jit_solution(14616134283706953128)
XLA Ops:
  6.5 0.0 copy-start
  6.5 0.0 copy-start.1
  6.5 0.0 all-gather.3.cloned.1.call-start
  6.5 0.7 all-gather.3.cloned.1.call-update
  7.3 1.4 %convert_reduce_fusion.1 = f32[224]{0:T(256)S(1)} fusion(bf16[2048,224]{0,1:T(8,128)(2,1)} %param.7), kind=kLoop, calls=%fused_computation.6 | loop fusion | flops 1376032 | bytes 918400 | tf_op jit(solution)/shard_map/reduce_sum | solution.py:26
  8.7 0.1 broadcast_in_dim.41
  8.8 1.2 %broadcast_maximum_fusion = bf16[2048,224]{0,1:T(8,128)(2,1)S(1)} fusion(bf16[2048,224]{0,1:T(8,128)(2,1)} %param.6), kind=kLoop, calls=%fused_computation.16 | loop fusion | flops 458752 | bytes 1835008 | tf_op jit(solution)/shard_map/max | solution.py:18
  10.0 0.7 reshape.48
  10.7 3.2 %reshape.47 = bf16[4,512,2,112]{1,0,3,2:T(4,128)(2,1)} reshape(bf16[2048,224]{0,1:T(8,128)(2,1)} %param.8) | data formatting | bytes 1835008 | tf_op jit(solution)/shard_map/reshape | solution.py:20
  13.9 0.0 copy-done.1
  13.9 0.1 broadcast_maximum_fusion.1
  14.0 0.7 reshape.46
  14.7 0.4 convert_reduce_fusion
  15.1 0.4 reduce_window_sum.23
  15.5 13.3 %all_gather.10 = f32[4,2,112]{2,1,0:T(2,128)S(1)} all-gather(f32[1,2,112]{2,1,0:T(2,128)S(1)} %broadcast_in_dim.41), channel_id=1, replica_groups=mesh['groups'=2,'frames'=4,'heads'=4] {'frames'}, dimensions={0}, use_global_device_ids=true | all-gather | bytes 4480 | tf_op jit(solution)/shard_map/all_gather | solution.py:30
  28.8 0.1 select_reduce_fusion.1
  28.9 0.1 fusion.12
  29.0 0.1 copy.16
  29.1 1.8 %fusion.17 = (f32[2,112,112]{2,1,0:T(8,128)S(1)}, f32[4,2,112,112]{3,2,1,0:T(8,128)S(1)}) fusion(bf16[4,512,2,112]{1,0,3,2:T(4,128)(2,1)} %reshape.47, bf16[4,512,2,112]{1,0,3,2:T(4,128)(2,1)S(1)} %reshape.46), kind=kOutput, calls=%fused_computation.36 | convolution fusion | flops 102835712 | bytes 2336768 | tf_op jit(solution)/shard_map/fthi,fthj->fhij/dot_general | solution.py:21
  30.9 19.9 %all-gather = f32[8,112,112]{2,1,0:T(8,128)S(1)} all-gather(f32[2,112,112]{2,1,0:T(8,128)S(1)} %get-tuple-element.5), channel_id=2, replica_groups=mesh['groups'=2,'frames'=4,'heads'=4] {'frames'}, dimensions={0}, use_global_device_ids=true | all-gather | bytes 501760 | tf_op jit(solution)/shard_map/all_gather | solution.py:29
  50.8 0.1 select_reduce_fusion
  50.9 0.4 fusion.7
  51.3 0.1 fusion.3
  51.3 1.4 %fusion.2 = bf16[4,512,2,112]{1,3,2,0:T(8,128)(2,1)} fusion(bf16[4,2,112,112]{3,2,1,0:T(8,128)(2,1)S(1)} %fusion.3, f32[4,512,2]{1,2,0:T(2,128)S(1)} %fusion.13, bf16[4,512,2,112]{1,0,3,2:T(4,128)(2,1)S(1)} %reshape.48), kind=kOutput, calls=%fused_computation.4 | convolution fusion | flops 103677952 | bytes 2052096 | tf_op jit(solution)/shard_map/fthi,fhij->fthj/dot_general | solution.py:40
  52.7 0.0 copy-start.2
  52.7 3.6 %all-to-all-start = ((bf16[4,512,224]{1,2,0:T(8,128)(2,1)}), bf16[4,512,224]{1,2,0:T(8,128)(2,1)S(1)}, u32[]{:S(2)}, u32[]{:S(2)}) async-start(bf16[4,512,224]{1,2,0:T(8,128)(2,1)} %bitcast.5), calls=%async_computation | async-start | bytes 1835008 | tf_op jit(solution)/shard_map/all_to_all | solution.py:59
  56.4 0.0 copy-done
  56.4 4.1 %fusion.10 = f32[512,2240]{0,1:T(8,128)} fusion(f32[4,2240]{1,0:T(4,128)S(1)} %copy-done, s32[512]{0:T(512)S(1)} %add_select_fusion), kind=kOutput, calls=%fused_computation.19 | convolution fusion | flops 55052288 | bytes 4625408 | tf_op jit(solution)/shard_map/dot_general | solution.py:56
  60.5 8.8 %all-to-all-done = bf16[4,512,224]{1,2,0:T(8,128)(2,1)S(1)} async-done(((bf16[4,512,224]{1,2,0:T(8,128)(2,1)}), bf16[4,512,224]{1,2,0:T(8,128)(2,1)S(1)}, u32[]{:S(2)}, u32[]{:S(2)}) %all-to-all-start) | async-done | bytes 917536 | tf_op jit(solution)/shard_map/all_to_all | solution.py:59
  69.4 29.2 %all-gather.3.cloned.1.call-done = bf16[896,2240]{1,0:T(8,128)(2,1)} async-done(((bf16[224,2240]{1,0:T(8,128)(2,1)}), bf16[896,2240]{1,0:T(8,128)(2,1)}) %all-gather.3.cloned.1.call-update) | async-done | bytes 4014096 | tf_op jit(solution)/shard_map/all_gather | solution.py:62
  98.6 0.0 copy-done.2
  98.6 7.8 %fusion.1 = bf16[512,2240]{0,1:T(8,128)(2,1)} fusion(f32[512,2240]{0,1:T(8,128)} %fusion.10, bf16[512,896]{0,1:T(8,128)(2,1)S(1)} %bitcast.30, bf16[896,2240]{1,0:T(8,128)(2,1)} %all-gather.3.cloned.1.call-done, bf16[512,2240]{0,1:T(8,128)(2,1)S(1)} %copy-done.2), kind=kOutput, calls=%fused_computation.2 | convolution fusion | flops 2059796480 | bytes 14106624 | tf_op jit(solution)/shard_map/dot_general | solution.py:60
  (3 shorter events, 0.0 us)
Async XLA Ops:
  6.5 49.9 %copy-start = (f32[4,2240]{1,0:T(4,128)S(1)}, f32[4,2240]{1,0:T(4,128)}, u32[]{:S(2)}) copy-start(f32[4,2240]{1,0:T(4,128)} %param.11) | copy-start | bytes 107524
  6.5 7.4 %copy-start.1 = (bf16[2048,224]{0,1:T(8,128)(2,1)S(1)}, bf16[2048,224]{0,1:T(8,128)(2,1)}, u32[]{:S(2)}) copy-start(bf16[2048,224]{0,1:T(8,128)(2,1)} %param.7) | copy-start | bytes 2752516
  6.5 92.0 %all-gather.3.cloned.1.call-start = ((), (), s32[]{:S(2)}) async-start(), calls=%async_computation.1 | async-start | bytes 5160960 | tf_op jit(solution)/shard_map/all_gather | solution.py:62
  52.7 45.9 %copy-start.2 = (bf16[512,2240]{0,1:T(8,128)(2,1)S(1)}, bf16[512,2240]{0,1:T(8,128)(2,1)}, u32[]{:S(2)}) copy-start(bf16[512,2240]{0,1:T(8,128)(2,1)} %param.9) | copy-start | bytes 6881284
  52.7 16.6 %all-to-all-start = ((bf16[4,512,224]{1,2,0:T(8,128)(2,1)}), bf16[4,512,224]{1,2,0:T(8,128)(2,1)S(1)}, u32[]{:S(2)}, u32[]{:S(2)}) async-start(bf16[4,512,224]{1,2,0:T(8,128)(2,1)} %bitcast.5), calls=%async_computation | async-start | bytes 1835008 | tf_op jit(solution)/shard_map/all_to_all | solution.py:59
Sparse Core Ops, SparseCore 0:
  8.9 89.6 all-gather.2
where the time goes:
time: 114 us; the launch traced here: 113 us
  waiting for transfers between devices  38.8 us (34%)
  blocking collectives  33.1 us (29%)
  matrix products  15.5 us (14%)
  between operations  13.5 us (12%)
  local copies, waits for them, and re-layouts  4.76 us (4%)
  other arithmetic  3.95 us (3%)
  starting transfers between devices  3.64 us (3%)
    all_gather x1, waiting for transfers between devices, per_device(): lax.all_gather(out_proj, 'frames', axis=0, tiled=True)  29.2 us
    all_gather x1, blocking collectives, per_device(): lax.all_gather(own_state[None], 'frames', axis=0, tiled=True)  19.9 us
    all_gather x1, blocking collectives, per_device(): lax.all_gather(own_sum[None], 'frames', axis=0, tiled=True)  13.3 us
    all_to_all x1, waiting for transfers between devices, per_device(): lax.all_to_all(attended, 'heads', split_axis=0, concat_axis=1, tiled=True)  8.84 us
    dot_general x1, matrix products, per_device(): jnp.dot(token_rows, lax.all_gather(out_proj, 'frames', axis=0, tiled=True...  7.75 us
    dot_general x1, matrix products, per_device(): jnp.dot(selector, frame_gate, precision=lax.Precision.HIGHEST, preferred_...  4.13 us
    all_to_all x1, starting transfers between devices, per_device(): lax.all_to_all(attended, 'heads', split_axis=0, concat_axis=1, tiled=True)  3.64 us
    reshape x1, local copies, waits for them, and re-layouts, per_device(): value_frames = value_heads.reshape(block_shape)  3.23 us
  transfers between devices with their start and end apart: 2, of which 2 were waited for; matrix products, arithmetic and copies ran while one was open for 14% of the time, Pallas kernels for 0%

commit v1 on v0

v1 whole, which is shorter than its diff:
```python
import jax
import jax.numpy as jnp
from jax import lax
from jax.sharding import PartitionSpec as P

HD = 112
FRAME_TOK = 512


EPSILON = 1e-06


def _exclusive_prefix(x, nf):
    if nf <= 8:
        total = jnp.zeros_like(x)
        for d in range(1, nf):
            total = total + lax.ppermute(x, "frames", [(i, i + d) for i in range(nf - d)])
        return total
    y = lax.ppermute(x, "frames", [(i, i + 1) for i in range(nf - 1)])
    covered = 1
    while covered < nf - 1:
        y = y + lax.ppermute(y, "frames", [(i, i + covered) for i in range(nf - covered)])
        covered *= 2
    return y


def _gather_out_proj(out_proj, nf, nh):
    rows, cols = out_proj.shape
    half = rows // 2
    j = lax.axis_index("frames")
    core = lax.axis_index("heads") % 2
    mine = lax.dynamic_slice_in_dim(out_proj, core * half, half, axis=0)
    swap = [(a, a ^ 1) for a in range(nh)]
    buf = jnp.zeros((nf, 2, half, cols), out_proj.dtype)
    buf = lax.dynamic_update_slice(buf, out_proj.reshape(1, 2, half, cols), (j, 0, 0, 0))
    left = mine
    right = mine
    for t in range(1, nf):
        left = lax.ppermute(left, "frames", [(i, i + 1) for i in range(t - 1, nf - 1)])
        right = lax.ppermute(right, "frames", [(i, i - 1) for i in range(1, nf - t + 1)])
        for piece, block in ((left, j - t), (right, j + t)):
            other = lax.ppermute(piece, "heads", swap)
            slot = jnp.remainder(block, nf)
            for part, side in ((piece, core), (other, 1 - core)):
                cur = lax.dynamic_slice(buf, (slot, side, 0, 0), (1, 1, half, cols))
                buf = lax.dynamic_update_slice(
                    buf, cur + part.reshape(1, 1, half, cols), (slot, side, 0, 0)
                )
    return buf.reshape(nf * rows, cols)


def make_per_device(nf, nh):
    def per_device(query_heads, key_heads, value_heads, residual, out_proj, frame_gate):
        length, width = query_heads.shape
        frames_here = length // FRAME_TOK
        heads_here = width // HD
        block_shape = (frames_here, FRAME_TOK, width)
        query_pos = jnp.maximum(query_heads, 0).reshape(block_shape)
        key_pos = jnp.maximum(key_heads, 0).reshape(block_shape)
        value_frames = value_heads.reshape(block_shape)
        lane_head = jnp.arange(width, dtype=jnp.int32) // HD
        same_head = lane_head[:, None] == lane_head[None, :]

        frame_state = jnp.einsum(
            "fti,ftj->fij", key_pos, value_frames, preferred_element_type=jnp.float32
        )
        frame_state = jnp.where(same_head[None], frame_state, 0.0)
        frame_sum = jnp.sum(key_pos, axis=1, dtype=jnp.float32)
        own_state = jnp.sum(frame_state, axis=0)
        own_sum = jnp.sum(frame_sum, axis=0)

        blocks = [
            own_state[a * HD:(a + 1) * HD, a * HD:(a + 1) * HD] for a in range(heads_here)
        ]
        compact = jnp.concatenate(
            [jnp.stack(blocks), own_sum.reshape(heads_here, 1, HD)], axis=1
        )
        earlier = _exclusive_prefix(compact, nf)
        eye = jnp.eye(heads_here, dtype=jnp.float32)
        earlier_state = jnp.einsum(
            "aij,ab->aibj", earlier[:, :HD, :], eye, precision=lax.Precision.HIGHEST
        ).reshape(width, width)
        earlier_sum = earlier[:, HD, :].reshape(width)

        prefix_state = earlier_state[None] + jnp.cumsum(frame_state, axis=0)
        prefix_sum = earlier_sum[None] + jnp.cumsum(frame_sum, axis=0)
        state_round = prefix_state.astype(jnp.bfloat16)
        sum_round = prefix_sum.astype(jnp.bfloat16)
        sum_matrix = jnp.where(same_head[None], sum_round[:, :, None], jnp.zeros((), jnp.bfloat16))
        numerator = jnp.einsum(
            "fti,fij->ftj", query_pos, state_round, preferred_element_type=jnp.float32
        )
        denominator = (
            jnp.einsum("fti,fij->ftj", query_pos, sum_matrix, preferred_element_type=jnp.float32)
            + EPSILON
        )
        attended = (numerator / denominator).astype(jnp.bfloat16).reshape(length, width)

        weights = _gather_out_proj(out_proj, nf, nh)

        rows_here = residual.shape[0]
        head_pos = lax.axis_index("heads")
        if rows_here <= FRAME_TOK and FRAME_TOK % rows_here == 0:
            gate_rows = lax.dynamic_slice_in_dim(
                frame_gate, (head_pos * rows_here) // FRAME_TOK, 1, axis=0
            )
        else:
            row_frame = (head_pos * rows_here + jnp.arange(rows_here, dtype=jnp.int32)) // FRAME_TOK
            gate_rows = jnp.take(frame_gate, row_frame, axis=0)
        token_rows = lax.all_to_all(attended, "heads", split_axis=0, concat_axis=1, tiled=True)
        projected = jnp.dot(token_rows, weights, preferred_element_type=jnp.float32)
        return (residual.astype(jnp.float32) + gate_rows * projected).astype(jnp.bfloat16)

    return per_device


def solution(mesh):
    nf = mesh.shape["frames"]
    nh = mesh.shape["heads"]
    in_specs = (
        P(("groups", "frames"), "heads"),
        P(("groups", "frames"), "heads"),
        P(("groups", "frames"), "heads"),
        P(("groups", "frames", "heads"), None),
        P("frames", None),
        P(("groups", "frames"), None),
    )
    out_specs = P(("groups", "frames", "heads"), None)
    return jax.shard_map(
        make_per_device(nf, nh), mesh=mesh, in_specs=in_specs, out_specs=out_specs, check_vma=False
    )
```

time: 114 us -> 96.4 us (0.85)
  blocking collectives: 33.1 us -> 0 us
  other arithmetic: 3.95 us -> 32.3 us
  starting transfers between devices: 3.64 us -> 27.7 us
  waiting for transfers between devices: 38.8 us -> 17.8 us
  between operations: 13.5 us -> 0.19 us
  matrix products: 15.5 us -> 11.8 us
    all_gather x2 -> x0, blocking collectives: 33.1 us -> none  [the longest x1 19.9 us: per_device(): lax.all_gather(own_state[None], 'frames', axis=0, tiled=True)]
    all_gather x1 -> x0, waiting for transfers between devices: 29.2 us -> none  [per_device(): lax.all_gather(out_proj, 'frames', axis=0, tiled=True)]
    ppermute x0 -> x15, starting transfers between devices: none -> 24.2 us  [the longest x3 11.6 us: _exclusive_prefix(): lax.ppermute(x, 'frames', [(i, i + d) for i in range(nf - d)])]
    dynamic_update_slice x0 -> x12, other arithmetic: none -> 24 us  [_gather_out_proj(): lax.dynamic_update_slice(buf, cur + part.reshape(1, 1, half, cols), (slot...]
    ppermute x0 -> x15, waiting for transfers between devices: none -> 17.8 us  [the longest x3 17.8 us: _gather_out_proj(): lax.ppermute(right, 'frames', [(i, i - 1) for i in range(1, nf - t + 1)])]
    all_to_all x1, waiting for transfers between devices: 8.84 us -> 0.01 us  [per_device(): lax.all_to_all(attended, 'heads', split_axis=0, concat_axis=1, tiled=True)]
    reshape x2 -> x1, local copies, waits for them, and re-layouts: 3.9 us -> 0.08 us  [per_device(): own_sum.reshape(heads_here, 1, HD)]
    dot_general x5 -> x4, matrix products: 15.5 us -> 11.8 us  [the longest x1 7.03 us: per_device(): projected = jnp.dot(token_rows, weights, preferred_element_type=jnp.float32)]
  transfers between devices with their start and end apart: 2 -> 16, of which waited for: 2 -> 2; matrix products, arithmetic and copies ran while one was open for 14% -> 44% of each run, Pallas kernels for 0% -> 0%
where the time goes in v1:
time: 96.4 us; the launch traced here: 95.3 us
  other arithmetic  32.3 us (34%)
  starting transfers between devices  27.7 us (29%)
  waiting for transfers between devices  17.8 us (18%)
  matrix products  11.8 us (12%)
  local copies, waits for them, and re-layouts  5.54 us (6%)
    dynamic_update_slice x12, other arithmetic, _gather_out_proj(): lax.dynamic_update_slice(buf, cur + part.reshape(1, 1, half, cols), (slot...  24 us
    ppermute x3, waiting for transfers between devices, _gather_out_proj(): lax.ppermute(right, 'frames', [(i, i - 1) for i in range(1, nf - t + 1)])  17.8 us
    ppermute x3, starting transfers between devices, _exclusive_prefix(): lax.ppermute(x, 'frames', [(i, i + d) for i in range(nf - d)])  11.6 us
    ppermute x3, starting transfers between devices, _gather_out_proj(): lax.ppermute(left, 'frames', [(i, i + 1) for i in range(t - 1, nf - 1)])  7.15 us
    dot_general x1, matrix products, per_device(): projected = jnp.dot(token_rows, weights, preferred_element_type=jnp.float32)  7.03 us
    ppermute x3, starting transfers between devices, _gather_out_proj(): lax.ppermute(right, 'frames', [(i, i - 1) for i in range(1, nf - t + 1)])  3.84 us
    all_to_all x1, starting transfers between devices, per_device(): lax.all_to_all(attended, 'heads', split_axis=0, concat_axis=1, tiled=True)  3.51 us
    dot_general x1, matrix products, per_device(): jnp.einsum('fti,ftj->fij', key_pos, value_frames, preferred_element_type=...  2.58 us
  transfers between devices with their start and end apart: 16, of which 2 were waited for; matrix products, arithmetic and copies ran while one was open for 44% of the time, Pallas kernels for 0%

profile of v1, /device:TPU:0, one launch (start us, length us, event | category | flops | bytes accessed | tf_op | source)
XLA Modules:
  0.0 95.3 jit_solution(6710771853344057767)
XLA Ops:
  0.0 1.1 %constant_dynamic-slice_fusion = bf16[112,2240]{1,0:T(8,128)(2,1)S(1)} fusion(bf16[224,2240]{1,0:T(8,128)(2,1)} %param.10, s32[]{:T(128)S(6)} %select_n.141), kind=kLoop, calls=%fused_computation.56 | loop fusion | bytes 1003524 | tf_op jit(solution)/shard_map/dynamic_slice | solution.py:32
  1.1 5.8 %collective-permute-start.3 = (bf16[112,2240]{1,0:T(8,128)(2,1)S(1)}, bf16[112,2240]{1,0:T(8,128)(2,1)}, u32[]{:S(2)}, u32[]{:S(2)}) collective-permute-start(bf16[112,2240]{1,0:T(8,128)(2,1)S(1)} %constant_dynamic-slice_fusion), channel_id=1, source_target_pairs={{0,4},{4,8},{8,12},{1,5},{5,9},{9,13},{2,6},{6,10},{10,14},{3,7},{... | collective-permute-start | bytes 1505288 | tf_op jit(solution)/shard_map/ppermute | solution.py:39
  6.9 1.3 %collective-permute-start.5 = (bf16[112,2240]{1,0:T(8,128)(2,1)S(1)}, bf16[112,2240]{1,0:T(8,128)(2,1)}, u32[]{:S(2)}, u32[]{:S(2)}) collective-permute-start(bf16[112,2240]{1,0:T(8,128)(2,1)S(1)} %constant_dynamic-slice_fusion), channel_id=1, source_target_pairs={{4,0},{8,4},{12,8},{5,1},{9,5},{13,9},{6,2},{10,6},{14,10},{7,3},{... | collective-permute-start | bytes 1505288 | tf_op jit(solution)/shard_map/ppermute | solution.py:40
  8.2 1.2 %broadcast_maximum_fusion = bf16[2048,224]{0,1:T(8,128)(2,1)S(1)} fusion(bf16[2048,224]{0,1:T(8,128)(2,1)} %param.7), kind=kLoop, calls=%fused_computation.43 | loop fusion | flops 458752 | bytes 1835008 | tf_op jit(solution)/shard_map/max | solution.py:59
  9.4 1.4 %convert_reduce_fusion.1 = f32[224]{0:T(256)S(1)} fusion(bf16[2048,224]{0,1:T(8,128)(2,1)} %param.7), kind=kLoop, calls=%fused_computation.5 | loop fusion | flops 1376032 | bytes 918400 | tf_op jit(solution)/shard_map/reduce_sum | solution.py:70
  11.0 2.6 %fusion.29 = (f32[224,224]{1,0:T(8,128)S(1)}, f32[4,224,224]{2,1,0:T(8,128)}) fusion(bf16[28,4,8,512]{3,2,1,0:T(8,128)(2,1)} %bitcast.88, bf16[28,4,8,512]{3,2,1,0:T(8,128)(2,1)S(1)} %bitcast.83, pred[224,224]{1,0:T(8,128)(4,1)S(1)} %broadcast_compare_fusion), kind=kOutput, calls=%fused_computation.65 | convolution fusion | flops 205872128 | bytes 2888704 | tf_op jit(solution)/shard_map/fti,ftj->fij/dot_general | solution.py:64
  14.4 5.2 %collective-permute-start = (f32[2,113,112]{2,1,0:T(8,128)}, f32[2,113,112]{2,1,0:T(8,128)}, u32[]{:S(2)}, u32[]{:S(2)}) collective-permute-start(f32[2,113,112]{2,1,0:T(8,128)} %pad_maximum_fusion), channel_id=1, source_target_pairs={{0,4},{4,8},{8,12},{1,5},{5,9},{9,13},{2,6},{6,10},{10,14},{3,7},{... | collective-permute-start | bytes 303752 | tf_op jit(solution)/shard_map/ppermute | solution.py:17
  19.6 4.5 %collective-permute-start.1 = (f32[2,113,112]{2,1,0:T(8,128)}, f32[2,113,112]{2,1,0:T(8,128)}, u32[]{:S(2)}, u32[]{:S(2)}) collective-permute-start(f32[2,113,112]{2,1,0:T(8,128)} %pad_maximum_fusion), channel_id=1, source_target_pairs={{0,8},{4,12},{1,9},{5,13},{2,10},{6,14},{3,11},{7,15},{16,24},{20,... | collective-permute-start | bytes 303752 | tf_op jit(solution)/shard_map/ppermute | solution.py:17
  24.1 1.9 %collective-permute-start.2 = (f32[2,113,112]{2,1,0:T(8,128)}, f32[2,113,112]{2,1,0:T(8,128)}, u32[]{:S(2)}, u32[]{:S(2)}) collective-permute-start(f32[2,113,112]{2,1,0:T(8,128)} %pad_maximum_fusion), channel_id=1, source_target_pairs={{0,12},{1,13},{2,14},{3,15},{16,28},{17,29},{18,30},{19,31}} | collective-permute-start | bytes 303752 | tf_op jit(solution)/shard_map/ppermute | solution.py:17
  26.7 1.2 %broadcast_maximum_fusion.1 = bf16[2048,224]{0,1:T(8,128)(2,1)S(1)} fusion(bf16[2048,224]{0,1:T(8,128)(2,1)} %param.6), kind=kLoop, calls=%fused_computation.44 | loop fusion | flops 458752 | bytes 1835008 | tf_op jit(solution)/shard_map/max | solution.py:58
  27.9 1.1 %convert_reduce_fusion = f32[4,224]{0,1:T(8,128)} fusion(bf16[4,512,224]{1,0,2:T(4,128)(2,1)S(1)} %reshape.136), kind=kLoop, calls=%fused_computation.4 | loop fusion | flops 916608 | bytes 921088 | tf_op jit(solution)/shard_map/reduce_sum | solution.py:68
  29.0 1.2 %reduce_window_sum.23 = f32[4,224]{0,1:T(8,128)S(1)} reduce-window(f32[4,224]{0,1:T(8,128)} %convert_reduce_fusion, f32[]{:T(128)} %constant.90.clone.1), window={size=4x1 pad=3_0x0_0}, to_apply=%region_4.5 | reduce-window | flops 2688 | bytes 7172 | tf_op jit(solution)/shard_map/jit(cumsum)/reduce_window_sum | solution.py:86
  30.2 2.2 %broadcast_in_dim.44 = bf16[4,2,112,2240]{3,2,1,0:T(8,128)(2,1)} broadcast(bf16[]{:T(256)} %constant.88.clone.1), dimensions={} | broadcast | bytes 4014082 | tf_op jit(solution)/shard_map/broadcast_in_dim | solution.py:34
  35.7 1.6 %divide_convert_fusion = bf16[4,512,224]{1,2,0:T(8,128)(2,1)} fusion(f32[4,512,224]{1,2,0:T(8,128)S(1)} %fusion.8, bf16[28,4,8,512]{3,2,1,0:T(8,128)(2,1)S(1)} %bitcast.85, pred[224,224]{1,0:T(8,128)(4,1)S(1)} %copy-done.4, bf16[4,224]{1,0:T(4,128)(2,1)S(1)} %copy.17), kind=kOutput, calls=%fused_computation.3 | convolution fusion | flops 207097856 | bytes 3721984 | tf_op jit(solution)/shard_map/fti,fij->ftj/dot_general | solution.py:94
  37.4 3.5 %all-to-all-start = ((bf16[4,512,224]{1,2,0:T(8,128)(2,1)}), bf16[4,512,224]{1,2,0:T(8,128)(2,1)S(1)}, u32[]{:S(2)}, u32[]{:S(2)}) async-start(bf16[4,512,224]{1,2,0:T(8,128)(2,1)} %divide_convert_fusion), calls=%async_computation | async-start | bytes 1835008 | tf_op jit(solution)/shard_map/all_to_all | solution.py:110
  42.2 1.3 %collective-permute-start.9 = (bf16[112,2240]{1,0:T(8,128)(2,1)}, bf16[112,2240]{1,0:T(8,128)(2,1)S(1)}, u32[]{:S(2)}, u32[]{:S(2)}) collective-permute-start(bf16[112,2240]{1,0:T(8,128)(2,1)} %collective-permute-done.5), channel_id=1, source_target_pairs={{4,0},{8,4},{5,1},{9,5},{6,2},{10,6},{7,3},{11,7},{20,16},{24,20},... | collective-permute-start | bytes 1505288 | tf_op jit(solution)/shard_map/ppermute | solution.py:40
  43.5 2.1 %fusion.23 = bf16[4,2,112,2240]{3,2,1,0:T(8,128)(2,1)} fusion(bf16[4,2,112,2240]{3,2,1,0:T(8,128)(2,1)} %constant_dynamic-update-slice_fusion, s32[]{:T(128)S(6)} %select_n.138, s32[]{:T(128)S(6)} %select_n.140, bf16[112,2240]{1,0:T(8,128)(2,1)} %collective-permute-done.3), kind=kLoop, calls=%fused_computation.41 | loop fusion | flops 1003520 | bytes 1548296 | tf_op jit(solution)/shard_map/dynamic_update_slice | solution.py:46
  46.8 11.6 %collective-permute-done.9 = bf16[112,2240]{1,0:T(8,128)(2,1)S(1)} collective-permute-done((bf16[112,2240]{1,0:T(8,128)(2,1)}, bf16[112,2240]{1,0:T(8,128)(2,1)S(1)}, u32[]{:S(2)}, u32[]{:S(2)}) %collective-permute-start.9) | collective-permute-done | bytes 501792 | tf_op jit(solution)/shard_map/ppermute | solution.py:40
  58.4 1.3 %collective-permute-start.13 = (bf16[112,2240]{1,0:T(8,128)(2,1)S(1)}, bf16[112,2240]{1,0:T(8,128)(2,1)S(1)}, u32[]{:S(2)}, u32[]{:S(2)}) collective-permute-start(bf16[112,2240]{1,0:T(8,128)(2,1)S(1)} %collective-permute-done.9), channel_id=1, source_target_pairs={{4,0},{5,1},{6,2},{7,3},{20,16},{21,17},{22,18},{23,19}} | collective-permute-start | bytes 1505288 | tf_op jit(solution)/shard_map/ppermute | solution.py:40
  59.7 2.0 %fusion.22 = bf16[4,2,112,2240]{3,2,1,0:T(8,128)(2,1)} fusion(bf16[4,2,112,2240]{3,2,1,0:T(8,128)(2,1)} %fusion.23, s32[]{:T(128)S(6)} %select_n.138, s32[]{:T(128)S(6)} %select_n.142, bf16[112,2240]{1,0:T(8,128)(2,1)S(1)} %collective-permute-done.4), kind=kLoop, calls=%fused_computation.39 | loop fusion | flops 1003520 | bytes 1533960 | tf_op jit(solution)/shard_map/dynamic_update_slice | solution.py:46
  61.7 2.1 %fusion.21 = bf16[4,2,112,2240]{3,2,1,0:T(8,128)(2,1)} fusion(bf16[4,2,112,2240]{3,2,1,0:T(8,128)(2,1)} %fusion.22, s32[]{:T(128)S(6)} %select_n.144, s32[]{:T(128)S(6)} %select_n.140, bf16[112,2240]{1,0:T(8,128)(2,1)} %collective-permute-done.5), kind=kLoop, calls=%fused_computation.37 | loop fusion | flops 1003520 | bytes 1548296 | tf_op jit(solution)/shard_map/dynamic_update_slice | solution.py:46
  63.8 2.0 %fusion.20 = bf16[4,2,112,2240]{3,2,1,0:T(8,128)(2,1)} fusion(bf16[4,2,112,2240]{3,2,1,0:T(8,128)(2,1)} %fusion.21, s32[]{:T(128)S(6)} %select_n.144, s32[]{:T(128)S(6)} %select_n.142, bf16[112,2240]{1,0:T(8,128)(2,1)S(1)} %collective-permute-done.6), kind=kLoop, calls=%fused_computation.35 | loop fusion | flops 1003520 | bytes 1533960 | tf_op jit(solution)/shard_map/dynamic_update_slice | solution.py:46
  65.8 2.0 %fusion.19 = bf16[4,2,112,2240]{3,2,1,0:T(8,128)(2,1)} fusion(bf16[4,2,112,2240]{3,2,1,0:T(8,128)(2,1)} %fusion.20, s32[]{:T(128)S(6)} %select_n.146, s32[]{:T(128)S(6)} %select_n.140, bf16[112,2240]{1,0:T(8,128)(2,1)S(1)} %collective-permute-done.7), kind=kLoop, calls=%fused_computation.33 | loop fusion | flops 1003520 | bytes 1533960 | tf_op jit(solution)/shard_map/dynamic_update_slice | solution.py:46
  68.3 6.2 %collective-permute-done.13 = bf16[112,2240]{1,0:T(8,128)(2,1)S(1)} collective-permute-done((bf16[112,2240]{1,0:T(8,128)(2,1)S(1)}, bf16[112,2240]{1,0:T(8,128)(2,1)S(1)}, u32[]{:S(2)}, u32[]{:S(2)}) %collective-permute-start.13) | collective-permute-done | bytes 501792 | tf_op jit(solution)/shard_map/ppermute | solution.py:40
  74.4 2.0 %fusion.18 = bf16[4,2,112,2240]{3,2,1,0:T(8,128)(2,1)} fusion(bf16[4,2,112,2240]{3,2,1,0:T(8,128)(2,1)} %fusion.19, s32[]{:T(128)S(6)} %select_n.146, s32[]{:T(128)S(6)} %select_n.142, bf16[112,2240]{1,0:T(8,128)(2,1)S(1)} %collective-permute-done.8), kind=kLoop, calls=%fused_computation.31 | loop fusion | flops 1003520 | bytes 1533960 | tf_op jit(solution)/shard_map/dynamic_update_slice | solution.py:46
  76.4 2.0 %fusion.17 = bf16[4,2,112,2240]{3,2,1,0:T(8,128)(2,1)} fusion(bf16[4,2,112,2240]{3,2,1,0:T(8,128)(2,1)} %fusion.18, s32[]{:T(128)S(6)} %select_n.148, s32[]{:T(128)S(6)} %select_n.140, bf16[112,2240]{1,0:T(8,128)(2,1)S(1)} %collective-permute-done.9), kind=kLoop, calls=%fused_computation.29 | loop fusion | flops 1003520 | bytes 1533960 | tf_op jit(solution)/shard_map/dynamic_update_slice | solution.py:46
  78.4 2.0 %fusion.16 = bf16[4,2,112,2240]{3,2,1,0:T(8,128)(2,1)} fusion(bf16[4,2,112,2240]{3,2,1,0:T(8,128)(2,1)} %fusion.17, s32[]{:T(128)S(6)} %select_n.148, s32[]{:T(128)S(6)} %select_n.142, bf16[112,2240]{1,0:T(8,128)(2,1)S(1)} %collective-permute-done.10), kind=kLoop, calls=%fused_computation.27 | loop fusion | flops 1003520 | bytes 1533960 | tf_op jit(solution)/shard_map/dynamic_update_slice | solution.py:46
  80.4 2.0 %fusion.15 = bf16[4,2,112,2240]{3,2,1,0:T(8,128)(2,1)} fusion(bf16[4,2,112,2240]{3,2,1,0:T(8,128)(2,1)} %fusion.16, s32[]{:T(128)S(6)} %select_n.150, s32[]{:T(128)S(6)} %select_n.140, bf16[112,2240]{1,0:T(8,128)(2,1)S(1)} %collective-permute-done.11), kind=kLoop, calls=%fused_computation.25 | loop fusion | flops 1003520 | bytes 1533960 | tf_op jit(solution)/shard_map/dynamic_update_slice | solution.py:46
  82.3 2.0 %fusion.14 = bf16[4,2,112,2240]{3,2,1,0:T(8,128)(2,1)} fusion(bf16[4,2,112,2240]{3,2,1,0:T(8,128)(2,1)} %fusion.15, s32[]{:T(128)S(6)} %select_n.150, s32[]{:T(128)S(6)} %select_n.142, bf16[112,2240]{1,0:T(8,128)(2,1)S(1)} %collective-permute-done.12), kind=kLoop, calls=%fused_computation.23 | loop fusion | flops 1003520 | bytes 1533960 | tf_op jit(solution)/shard_map/dynamic_update_slice | solution.py:46
  84.3 2.0 %fusion.13 = bf16[4,2,112,2240]{3,2,1,0:T(8,128)(2,1)} fusion(bf16[4,2,112,2240]{3,2,1,0:T(8,128)(2,1)} %fusion.14, s32[]{:T(128)S(6)} %select_n.152, s32[]{:T(128)S(6)} %select_n.140, bf16[112,2240]{1,0:T(8,128)(2,1)S(1)} %collective-permute-done.13), kind=kLoop, calls=%fused_computation.21 | loop fusion | flops 1003520 | bytes 1533960 | tf_op jit(solution)/shard_map/dynamic_update_slice | solution.py:46
  86.3 2.0 %fusion.12 = bf16[4,2,112,2240]{3,2,1,0:T(8,128)(2,1)} fusion(bf16[4,2,112,2240]{3,2,1,0:T(8,128)(2,1)} %fusion.13, s32[]{:T(128)S(6)} %select_n.152, s32[]{:T(128)S(6)} %select_n.142, bf16[112,2240]{1,0:T(8,128)(2,1)S(1)} %collective-permute-done.14), kind=kLoop, calls=%fused_computation.19 | loop fusion | flops 1003520 | bytes 1533960 | tf_op jit(solution)/shard_map/dynamic_update_slice | solution.py:46
  88.3 7.0 %fusion.1 = bf16[512,2240]{0,1:T(8,128)(2,1)} fusion(bf16[512,896]{0,1:T(8,128)(2,1)S(1)} %bitcast.87, bf16[896,2240]{1,0:T(8,128)(2,1)} %bitcast.18, bf16[512,2240]{0,1:T(8,128)(2,1)} %param.9, f32[2240]{0:T(1024)S(1)} %dynamic-slice_reduce_fusion), kind=kOutput, calls=%fused_computation.2 | convolution fusion | flops 2059796480 | bytes 9528064 | tf_op jit(solution)/shard_map/dot_general | solution.py:111
  (51 shorter events, 7.9 us)
Async XLA Ops:
  0.0 29.0 %copy-start = (f32[4,2240]{1,0:T(4,128)S(1)}, f32[4,2240]{1,0:T(4,128)}, u32[]{:S(2)}) copy-start(f32[4,2240]{1,0:T(4,128)} %param.11) | copy-start | bytes 107524
  1.1 39.8 %collective-permute-start.3 = (bf16[112,2240]{1,0:T(8,128)(2,1)S(1)}, bf16[112,2240]{1,0:T(8,128)(2,1)}, u32[]{:S(2)}, u32[]{:S(2)}) collective-permute-start(bf16[112,2240]{1,0:T(8,128)(2,1)S(1)} %constant_dynamic-slice_fusion), channel_id=1, source_target_pairs={{0,4},{4,8},{8,12},{1,5},{5,9},{9,13},{2,6},{6,10},{10,14},{3,7},{... | collective-permute-start | bytes 1505288 | tf_op jit(solution)/shard_map/ppermute | solution.py:39
  6.9 35.2 %collective-permute-start.5 = (bf16[112,2240]{1,0:T(8,128)(2,1)S(1)}, bf16[112,2240]{1,0:T(8,128)(2,1)}, u32[]{:S(2)}, u32[]{:S(2)}) collective-permute-start(bf16[112,2240]{1,0:T(8,128)(2,1)S(1)} %constant_dynamic-slice_fusion), channel_id=1, source_target_pairs={{4,0},{8,4},{12,8},{5,1},{9,5},{13,9},{6,2},{10,6},{14,10},{7,3},{... | collective-permute-start | bytes 1505288 | tf_op jit(solution)/shard_map/ppermute | solution.py:40
  11.0 2.6 %copy-start.3 = (pred[224,224]{1,0:T(8,128)(4,1)}, pred[224,224]{1,0:T(8,128)(4,1)S(1)}, u32[]{:S(2)}) copy-start(pred[224,224]{1,0:T(8,128)(4,1)S(1)} %broadcast_compare_fusion) | copy-start | bytes 150532
  14.4 19.1 %collective-permute-start = (f32[2,113,112]{2,1,0:T(8,128)}, f32[2,113,112]{2,1,0:T(8,128)}, u32[]{:S(2)}, u32[]{:S(2)}) collective-permute-start(f32[2,113,112]{2,1,0:T(8,128)} %pad_maximum_fusion), channel_id=1, source_target_pairs={{0,4},{4,8},{8,12},{1,5},{5,9},{9,13},{2,6},{6,10},{10,14},{3,7},{... | collective-permute-start | bytes 303752 | tf_op jit(solution)/shard_map/ppermute | solution.py:17
  19.6 13.9 %collective-permute-start.1 = (f32[2,113,112]{2,1,0:T(8,128)}, f32[2,113,112]{2,1,0:T(8,128)}, u32[]{:S(2)}, u32[]{:S(2)}) collective-permute-start(f32[2,113,112]{2,1,0:T(8,128)} %pad_maximum_fusion), channel_id=1, source_target_pairs={{0,8},{4,12},{1,9},{5,13},{2,10},{6,14},{3,11},{7,15},{16,24},{20,... | collective-permute-start | bytes 303752 | tf_op jit(solution)/shard_map/ppermute | solution.py:17
  24.1 9.4 %collective-permute-start.2 = (f32[2,113,112]{2,1,0:T(8,128)}, f32[2,113,112]{2,1,0:T(8,128)}, u32[]{:S(2)}, u32[]{:S(2)}) collective-permute-start(f32[2,113,112]{2,1,0:T(8,128)} %pad_maximum_fusion), channel_id=1, source_target_pairs={{0,12},{1,13},{2,14},{3,15},{16,28},{17,29},{18,30},{19,31}} | collective-permute-start | bytes 303752 | tf_op jit(solution)/shard_map/ppermute | solution.py:17
  26.0 6.4 %copy-start.1 = (bf16[224,2240]{1,0:T(8,128)(2,1)S(1)}, bf16[224,2240]{1,0:T(8,128)(2,1)}, u32[]{:S(2)}) copy-start(bf16[224,2240]{1,0:T(8,128)(2,1)} %param.10) | copy-start | bytes 3010564
  29.0 6.0 %copy-start.2 = (f32[4,224,224]{2,1,0:T(8,128)S(1)}, f32[4,224,224]{2,1,0:T(8,128)}, u32[]{:S(2)}) copy-start(f32[4,224,224]{2,1,0:T(8,128)} %get-tuple-element.8) | copy-start | bytes 2408452
  33.4 2.3 %copy-start.4 = (pred[224,224]{1,0:T(8,128)(4,1)S(1)}, pred[224,224]{1,0:T(8,128)(4,1)}, u32[]{:S(2)}) copy-start(pred[224,224]{1,0:T(8,128)(4,1)} %copy-done.3) | copy-start | bytes 150532
  37.4 50.9 %all-to-all-start = ((bf16[4,512,224]{1,2,0:T(8,128)(2,1)}), bf16[4,512,224]{1,2,0:T(8,128)(2,1)S(1)}, u32[]{:S(2)}, u32[]{:S(2)}) async-start(bf16[4,512,224]{1,2,0:T(8,128)(2,1)} %divide_convert_fusion), calls=%async_computation | async-start | bytes 1835008 | tf_op jit(solution)/shard_map/all_to_all | solution.py:110
  40.9 17.5 %collective-permute-start.4 = (bf16[112,2240]{1,0:T(8,128)(2,1)}, bf16[112,2240]{1,0:T(8,128)(2,1)S(1)}, u32[]{:S(2)}, u32[]{:S(2)}) collective-permute-start(bf16[112,2240]{1,0:T(8,128)(2,1)} %collective-permute-done.3), channel_id=1, source_target_pairs={{0,1},{1,0},{2,3},{3,2},{4,5},{5,4},{6,7},{7,6},{8,9},{9,8},{10,11... | collective-permute-start | bytes 1505288 | tf_op jit(solution)/shard_map/ppermute | solution.py:42
  41.4 4.3 %collective-permute-start.7 = (bf16[112,2240]{1,0:T(8,128)(2,1)}, bf16[112,2240]{1,0:T(8,128)(2,1)S(1)}, u32[]{:S(2)}, u32[]{:S(2)}) collective-permute-start(bf16[112,2240]{1,0:T(8,128)(2,1)} %collective-permute-done.3), channel_id=1, source_target_pairs={{4,8},{8,12},{5,9},{9,13},{6,10},{10,14},{7,11},{11,15},{20,24},{2... | collective-permute-start | bytes 1505288 | tf_op jit(solution)/shard_map/ppermute | solution.py:39
  42.1 21.7 %collective-permute-start.6 = (bf16[112,2240]{1,0:T(8,128)(2,1)}, bf16[112,2240]{1,0:T(8,128)(2,1)S(1)}, u32[]{:S(2)}, u32[]{:S(2)}) collective-permute-start(bf16[112,2240]{1,0:T(8,128)(2,1)} %collective-permute-done.5), channel_id=1, source_target_pairs={{0,1},{1,0},{2,3},{3,2},{4,5},{5,4},{6,7},{7,6},{8,9},{9,8},{10,11... | collective-permute-start | bytes 1505288 | tf_op jit(solution)/shard_map/ppermute | solution.py:42
  42.2 16.1 %collective-permute-start.9 = (bf16[112,2240]{1,0:T(8,128)(2,1)}, bf16[112,2240]{1,0:T(8,128)(2,1)S(1)}, u32[]{:S(2)}, u32[]{:S(2)}) collective-permute-start(bf16[112,2240]{1,0:T(8,128)(2,1)} %collective-permute-done.5), channel_id=1, source_target_pairs={{4,0},{8,4},{5,1},{9,5},{6,2},{10,6},{7,3},{11,7},{20,16},{24,20},... | collective-permute-start | bytes 1505288 | tf_op jit(solution)/shard_map/ppermute | solution.py:40
  45.6 28.8 %collective-permute-start.8 = (bf16[112,2240]{1,0:T(8,128)(2,1)S(1)}, bf16[112,2240]{1,0:T(8,128)(2,1)S(1)}, u32[]{:S(2)}, u32[]{:S(2)}) collective-permute-start(bf16[112,2240]{1,0:T(8,128)(2,1)S(1)} %collective-permute-done.7), channel_id=1, source_target_pairs={{0,1},{1,0},{2,3},{3,2},{4,5},{5,4},{6,7},{7,6},{8,9},{9,8},{10,11... | collective-permute-start | bytes 1505288 | tf_op jit(solution)/shard_map/ppermute | solution.py:42
  46.1 21.7 %collective-permute-start.11 = (bf16[112,2240]{1,0:T(8,128)(2,1)S(1)}, bf16[112,2240]{1,0:T(8,128)(2,1)S(1)}, u32[]{:S(2)}, u32[]{:S(2)}) collective-permute-start(bf16[112,2240]{1,0:T(8,128)(2,1)S(1)} %collective-permute-done.7), channel_id=1, source_target_pairs={{8,12},{9,13},{10,14},{11,15},{24,28},{25,29},{26,30},{27,31}} | collective-permute-start | bytes 1505288 | tf_op jit(solution)/shard_map/ppermute | solution.py:39
  58.4 20.0 %collective-permute-start.10 = (bf16[112,2240]{1,0:T(8,128)(2,1)S(1)}, bf16[112,2240]{1,0:T(8,128)(2,1)S(1)}, u32[]{:S(2)}, u32[]{:S(2)}) collective-permute-start(bf16[112,2240]{1,0:T(8,128)(2,1)S(1)} %collective-permute-done.9), channel_id=1, source_target_pairs={{0,1},{1,0},{2,3},{3,2},{4,5},{5,4},{6,7},{7,6},{8,9},{9,8},{10,11... | collective-permute-start | bytes 1505288 | tf_op jit(solution)/shard_map/ppermute | solution.py:42
  58.4 16.0 %collective-permute-start.13 = (bf16[112,2240]{1,0:T(8,128)(2,1)S(1)}, bf16[112,2240]{1,0:T(8,128)(2,1)S(1)}, u32[]{:S(2)}, u32[]{:S(2)}) collective-permute-start(bf16[112,2240]{1,0:T(8,128)(2,1)S(1)} %collective-permute-done.9), channel_id=1, source_target_pairs={{4,0},{5,1},{6,2},{7,3},{20,16},{21,17},{22,18},{23,19}} | collective-permute-start | bytes 1505288 | tf_op jit(solution)/shard_map/ppermute | solution.py:40
  67.8 14.6 %collective-permute-start.12 = (bf16[112,2240]{1,0:T(8,128)(2,1)S(1)}, bf16[112,2240]{1,0:T(8,128)(2,1)S(1)}, u32[]{:S(2)}, u32[]{:S(2)}) collective-permute-start(bf16[112,2240]{1,0:T(8,128)(2,1)S(1)} %collective-permute-done.11), channel_id=1, source_target_pairs={{0,1},{1,0},{2,3},{3,2},{4,5},{5,4},{6,7},{7,6},{8,9},{9,8},{10,11... | collective-permute-start | bytes 1505288 | tf_op jit(solution)/shard_map/ppermute | solution.py:42
  74.4 11.9 %collective-permute-start.14 = (bf16[112,2240]{1,0:T(8,128)(2,1)S(1)}, bf16[112,2240]{1,0:T(8,128)(2,1)S(1)}, u32[]{:S(2)}, u32[]{:S(2)}) collective-permute-start(bf16[112,2240]{1,0:T(8,128)(2,1)S(1)} %collective-permute-done.13), channel_id=1, source_target_pairs={{0,1},{1,0},{2,3},{3,2},{4,5},{5,4},{6,7},{7,6},{8,9},{9,8},{10,11... | collective-permute-start | bytes 1505288 | tf_op jit(solution)/shard_map/ppermute | solution.py:42

commit v2 on v1

--- a/solution.py
+++ b/solution.py
@@ -24,29 +24,22 @@
     return y
 
 
-def _gather_out_proj(out_proj, nf, nh):
+def _ring_out_proj(out_proj, nf, nh):
     rows, cols = out_proj.shape
     half = rows // 2
-    j = lax.axis_index("frames")
     core = lax.axis_index("heads") % 2
     mine = lax.dynamic_slice_in_dim(out_proj, core * half, half, axis=0)
+    theirs = lax.dynamic_slice_in_dim(out_proj, (1 - core) * half, half, axis=0)
+    ring = [(i, (i + 1) % nf) for i in range(nf)]
     swap = [(a, a ^ 1) for a in range(nh)]
-    buf = jnp.zeros((nf, 2, half, cols), out_proj.dtype)
-    buf = lax.dynamic_update_slice(buf, out_proj.reshape(1, 2, half, cols), (j, 0, 0, 0))
-    left = mine
-    right = mine
-    for t in range(1, nf):
-        left = lax.ppermute(left, "frames", [(i, i + 1) for i in range(t - 1, nf - 1)])
-        right = lax.ppermute(right, "frames", [(i, i - 1) for i in range(1, nf - t + 1)])
-        for piece, block in ((left, j - t), (right, j + t)):
-            other = lax.ppermute(piece, "heads", swap)
-            slot = jnp.remainder(block, nf)
-            for part, side in ((piece, core), (other, 1 - core)):
-                cur = lax.dynamic_slice(buf, (slot, side, 0, 0), (1, 1, half, cols))
-                buf = lax.dynamic_update_slice(
-                    buf, cur + part.reshape(1, 1, half, cols), (slot, side, 0, 0)
-                )
-    return buf.reshape(nf * rows, cols)
+    mine_pieces = [mine]
+    their_pieces = [theirs]
+    piece = mine
+    for _ in range(1, nf):
+        piece = lax.ppermute(piece, "frames", ring)
+        mine_pieces.append(piece)
+        their_pieces.append(lax.ppermute(piece, "heads", swap))
+    return jnp.stack(mine_pieces + their_pieces)
 
 
 def make_per_device(nf, nh):
@@ -96,7 +89,7 @@
         )
         attended = (numerator / denominator).astype(jnp.bfloat16).reshape(length, width)
 
-        weights = _gather_out_proj(out_proj, nf, nh)
+        weights = _ring_out_proj(out_proj, nf, nh)
 
         rows_here = residual.shape[0]
         head_pos = lax.axis_index("heads")
@@ -108,7 +101,17 @@
             row_frame = (head_pos * rows_here + jnp.arange(rows_here, dtype=jnp.int32)) // FRAME_TOK
             gate_rows = jnp.take(frame_gate, row_frame, axis=0)
         token_rows = lax.all_to_all(attended, "heads", split_axis=0, concat_axis=1, tiled=True)
-        projected = jnp.dot(token_rows, weights, preferred_element_type=jnp.float32)
+        rows_w, cols_w = out_proj.shape
+        half = rows_w // 2
+        by_half = token_rows.reshape(rows_here, nf * 2, half).transpose(1, 0, 2)
+        j = lax.axis_index("frames")
+        core = head_pos % 2
+        block = jnp.remainder(j - jnp.arange(nf, dtype=jnp.int32), nf)
+        order = jnp.concatenate([block * 2 + core, block * 2 + 1 - core])
+        matched = jnp.take(by_half, order, axis=0)
+        projected = jnp.einsum(
+            "ktr,krc->tc", matched, weights, preferred_element_type=jnp.float32
+        )
         return (residual.astype(jnp.float32) + gate_rows * projected).astype(jnp.bfloat16)
 
     return per_device

time: 96.4 us -> 78.1 us (0.81)
  other arithmetic: 32.3 us -> 8.77 us
  waiting for transfers between devices: 17.8 us -> 28.7 us
  starting transfers between devices: 27.7 us -> 16.9 us
  local copies, waits for them, and re-layouts: 5.54 us -> 11.1 us
    dynamic_update_slice x12 -> x0, other arithmetic: 24 us -> none  [_gather_out_proj(): lax.dynamic_update_slice(buf, cur + part.reshape(1, 1, half, cols), (slot...]
    ppermute x12 -> x6, starting transfers between devices: 12.6 us -> 1.76 us  [the longest x3 1.75 us: _ring_out_proj(): piece = lax.ppermute(piece, 'frames', ring)]
    all_to_all x1, waiting for transfers between devices: 0.01 us -> 8.78 us  [per_device(): lax.all_to_all(attended, 'heads', split_axis=0, concat_axis=1, tiled=True)]
    unnamed x10 -> x21, local copies, waits for them, and re-layouts: 0.02 us -> 8.17 us
    broadcast_in_dim x1 -> x0, local copies, waits for them, and re-layouts: 2.18 us -> none  [_gather_out_proj(): buf = jnp.zeros((nf, 2, half, cols), out_proj.dtype)]
    ppermute x12 -> x6, waiting for transfers between devices: 17.8 us -> 19.9 us  [the longest x3 19.9 us: _ring_out_proj(): piece = lax.ppermute(piece, 'frames', ring)]
    another operation x1, other arithmetic: 0.07 us -> 1.26 us  [per_device(): prefix_state = earlier_state[None] + jnp.cumsum(frame_state, axis=0)]
    max x1, other arithmetic: 1.24 us -> 0.06 us  [per_device(): query_pos = jnp.maximum(query_heads, 0).reshape(block_shape)]
  transfers between devices with their start and end apart: 16 -> 10, of which waited for: 2 -> 4; matrix products, arithmetic and copies ran while one was open for 44% -> 24% of each run, Pallas kernels for 0% -> 0%
where the time goes in v2:
time: 78.1 us; the launch traced here: 77.5 us
  waiting for transfers between devices  28.7 us (37%)
  starting transfers between devices  16.9 us (22%)
  matrix products  11.9 us (15%)
  local copies, waits for them, and re-layouts  11.1 us (14%)
  other arithmetic  8.77 us (11%)
    ppermute x3, waiting for transfers between devices, _ring_out_proj(): piece = lax.ppermute(piece, 'frames', ring)  19.9 us
    ppermute x3, starting transfers between devices, _exclusive_prefix(): lax.ppermute(x, 'frames', [(i, i + d) for i in range(nf - d)])  11.5 us
    all_to_all x1, waiting for transfers between devices, per_device(): lax.all_to_all(attended, 'heads', split_axis=0, concat_axis=1, tiled=True)  8.78 us
    unnamed x21, local copies, waits for them, and re-layouts  8.17 us
    dot_general x1, matrix products, per_device(): jnp.einsum('ktr,krc->tc', matched, weights, preferred_element_type=jnp.fl...  6.39 us
    all_to_all x1, starting transfers between devices, per_device(): lax.all_to_all(attended, 'heads', split_axis=0, concat_axis=1, tiled=True)  3.64 us
    dot_general x1, matrix products, per_device(): jnp.einsum('fti,ftj->fij', key_pos, value_frames, preferred_element_type=...  2.57 us
    dot_general x1, matrix products, per_device(): jnp.einsum('fti,fij->ftj', query_pos, sum_matrix, preferred_element_type=...  2.45 us
  transfers between devices with their start and end apart: 10, of which 4 were waited for; matrix products, arithmetic and copies ran while one was open for 24% of the time, Pallas kernels for 0%

profile of v2, /device:TPU:0, one launch (start us, length us, event | category | flops | bytes accessed | tf_op | source)
XLA Modules:
  0.0 77.5 jit_solution(2531182067581328277)
XLA Ops:
  0.0 1.3 %broadcast_maximum_fusion = bf16[2048,224]{0,1:T(8,128)(2,1)S(1)} fusion(bf16[2048,224]{0,1:T(8,128)(2,1)} %param.7), kind=kLoop, calls=%fused_computation.32 | loop fusion | flops 458752 | bytes 1835008 | tf_op jit(solution)/shard_map/max | solution.py:52
  1.4 1.5 %convert_reduce_fusion.1 = f32[224]{0:T(256)S(1)} fusion(bf16[2048,224]{0,1:T(8,128)(2,1)} %param.7), kind=kLoop, calls=%fused_computation.7 | loop fusion | flops 1376032 | bytes 918400 | tf_op jit(solution)/shard_map/reduce_sum | solution.py:63
  3.1 2.6 %fusion.25 = (f32[224,224]{1,0:T(8,128)S(1)}, f32[4,224,224]{2,1,0:T(8,128)}) fusion(bf16[28,4,8,512]{3,2,1,0:T(8,128)(2,1)} %bitcast.68, bf16[28,4,8,512]{3,2,1,0:T(8,128)(2,1)S(1)} %bitcast.63, pred[224,224]{1,0:T(8,128)(4,1)S(1)} %broadcast_compare_fusion), kind=kOutput, calls=%fused_computation.66 | convolution fusion | flops 205872128 | bytes 2888704 | tf_op jit(solution)/shard_map/fti,ftj->fij/dot_general | solution.py:57
  5.8 7.6 %collective-permute-start.2 = (f32[2,113,112]{2,1,0:T(8,128)S(1)}, f32[2,113,112]{2,1,0:T(8,128)}, u32[]{:S(2)}, u32[]{:S(2)}) collective-permute-start(f32[2,113,112]{2,1,0:T(8,128)S(1)} %pad_maximum_fusion), channel_id=1, source_target_pairs={{0,12},{1,13},{2,14},{3,15},{16,28},{17,29},{18,30},{19,31}} | collective-permute-start | bytes 303752 | tf_op jit(solution)/shard_map/ppermute | solution.py:17
  13.4 1.9 %collective-permute-start = (f32[2,113,112]{2,1,0:T(8,128)S(1)}, f32[2,113,112]{2,1,0:T(8,128)}, u32[]{:S(2)}, u32[]{:S(2)}) collective-permute-start(f32[2,113,112]{2,1,0:T(8,128)S(1)} %pad_maximum_fusion), channel_id=1, source_target_pairs={{0,4},{4,8},{8,12},{1,5},{5,9},{9,13},{2,6},{6,10},{10,14},{3,7},{... | collective-permute-start | bytes 303752 | tf_op jit(solution)/shard_map/ppermute | solution.py:17
  15.3 1.9 %collective-permute-start.1 = (f32[2,113,112]{2,1,0:T(8,128)S(1)}, f32[2,113,112]{2,1,0:T(8,128)}, u32[]{:S(2)}, u32[]{:S(2)}) collective-permute-start(f32[2,113,112]{2,1,0:T(8,128)S(1)} %pad_maximum_fusion), channel_id=1, source_target_pairs={{0,8},{4,12},{1,9},{5,13},{2,10},{6,14},{3,11},{7,15},{16,24},{20,... | collective-permute-start | bytes 303752 | tf_op jit(solution)/shard_map/ppermute | solution.py:17
  17.3 1.0 %bitcast_dynamic-update-slice_fusion.7 = (bf16[8,112,2240]{2,1,0:T(8,128)(2,1)}, bf16[112,2240]{1,0:T(8,128)(2,1)}) fusion(bf16[224,2240]{1,0:T(8,128)(2,1)S(1)} %copy-done.1, s32[]{:T(128)S(6)} %select_n.105), kind=kLoop, calls=%fused_computation.29 | loop fusion | bytes 1533956
  18.3 0.6 compare_convert_fusion
  18.9 0.7 reshape.161
  19.6 0.4 convert_reduce_fusion
  20.2 0.6 pad_clamp_fusion
  21.0 0.6 compare_and_fusion
  21.6 1.0 %add_add_fusion = f32[2,113,112]{2,1,0:T(8,128)S(1)} fusion(f32[2,113,112]{2,1,0:T(8,128)} %collective-permute-done.2, f32[2,113,112]{2,1,0:T(8,128)} %collective-permute-done, f32[2,113,112]{2,1,0:T(8,128)} %collective-permute-done.1), kind=kLoop, calls=%fused_computation.39 | loop fusion | flops 50624 | bytes 404992 | tf_op jit(solution)/shard_map/add | solution.py:17
  22.7 0.8 %multiply_bitcast_fusion = f32[2,112,2,112]{3,2,1,0:T(2,128)S(1)} fusion(f32[2,112,112]{2,1,0:T(8,128)S(1)} %slice.20, f32[2,2]{1,0:T(2,128)} %compare_convert_fusion), kind=kLoop, calls=%fused_computation.37 | loop fusion | flops 50176 | bytes 301072 | tf_op jit(solution)/shard_map/aij,ab->aibj/transpose | solution.py:73
  23.8 1.3 %fusion.3 = bf16[4,224,224]{2,1,0:T(8,128)(2,1)S(1)} fusion(f32[4,224,224]{2,1,0:T(8,128)} %get-tuple-element.10, f32[224,224]{1,0:T(8,128)S(1)} %add.150), kind=kOutput, calls=%fused_computation.10 | output fusion | flops 1003520 | bytes 1404928 | tf_op jit(solution)/shard_map/jit(cumsum)/reduce_window_sum | solution.py:78
  25.1 0.5 fusion.9
  25.8 2.4 %divide_convert_fusion = bf16[4,512,224]{1,2,0:T(8,128)(2,1)} fusion(f32[4,512,224]{1,2,0:T(8,128)S(1)} %fusion.9, bf16[28,4,8,512]{3,2,1,0:T(8,128)(2,1)S(1)} %bitcast.65, pred[224,224]{1,0:T(8,128)(4,1)} %copy-done.4, bf16[4,224]{1,0:T(4,128)(2,1)S(1)} %copy.17), kind=kOutput, calls=%fused_computation.5 | convolution fusion | flops 207097856 | bytes 3721984 | tf_op jit(solution)/shard_map/fti,fij->ftj/dot_general | solution.py:87
  28.2 3.6 %all-to-all-start = ((bf16[4,512,224]{1,2,0:T(8,128)(2,1)}), bf16[4,512,224]{1,2,0:T(8,128)(2,1)S(1)}, u32[]{:S(2)}, u32[]{:S(2)}) async-start(bf16[4,512,224]{1,2,0:T(8,128)(2,1)} %divide_convert_fusion), calls=%async_computation | async-start | bytes 1835008 | tf_op jit(solution)/shard_map/all_to_all | solution.py:103
  31.9 1.6 %collective-permute-done.3 = bf16[112,2240]{1,0:T(8,128)(2,1)S(1)} collective-permute-done((bf16[112,2240]{1,0:T(8,128)(2,1)}, bf16[112,2240]{1,0:T(8,128)(2,1)S(1)}, u32[]{:S(2)}, u32[]{:S(2)}) %collective-permute-start.3) | collective-permute-done | bytes 501792 | tf_op jit(solution)/shard_map/ppermute | solution.py:39
  33.5 1.7 %collective-permute-start.4 = (bf16[112,2240]{1,0:T(8,128)(2,1)S(1)}, bf16[112,2240]{1,0:T(8,128)(2,1)}, u32[]{:S(2)}, u32[]{:S(2)}) collective-permute-start(bf16[112,2240]{1,0:T(8,128)(2,1)S(1)} %collective-permute-done.3), channel_id=1, source_target_pairs={{0,4},{4,8},{8,12},{12,0},{1,5},{5,9},{9,13},{13,1},{2,6},{6,10},{... | collective-permute-start | bytes 1505288 | tf_op jit(solution)/shard_map/ppermute | solution.py:39
  35.2 0.8 %bitcast_dynamic-update-slice_fusion.6 = bf16[8,112,2240]{2,1,0:T(8,128)(2,1)} fusion(bf16[8,112,2240]{2,1,0:T(8,128)(2,1)} %get-tuple-element.5, bf16[112,2240]{1,0:T(8,128)(2,1)S(1)} %collective-permute-done.3), kind=kLoop, calls=%fused_computation.28 | loop fusion | bytes 1017856
  36.1 8.8 %all-to-all-done = bf16[4,512,224]{1,2,0:T(8,128)(2,1)S(1)} async-done(((bf16[4,512,224]{1,2,0:T(8,128)(2,1)}), bf16[4,512,224]{1,2,0:T(8,128)(2,1)S(1)}, u32[]{:S(2)}, u32[]{:S(2)}) %all-to-all-start) | async-done | bytes 917536 | tf_op jit(solution)/shard_map/all_to_all | solution.py:103
  44.9 0.9 %gather_fusion = bf16[8,512,112]{1,2,0:T(8,128)(2,1)S(1)} fusion(bf16[8,512,112]{1,2,0:T(8,128)(2,1)S(1)} %bitcast.62, s32[1024]{0:T(1024)} %pad_clamp_fusion), kind=kCustom, calls=%fused_computation | custom fusion | bytes 1835040 | tf_op jit(solution)/shard_map/jit(_take)/gather | solution.py:111
  45.7 4.7 %collective-permute-done.4 = bf16[112,2240]{1,0:T(8,128)(2,1)} collective-permute-done((bf16[112,2240]{1,0:T(8,128)(2,1)S(1)}, bf16[112,2240]{1,0:T(8,128)(2,1)}, u32[]{:S(2)}, u32[]{:S(2)}) %collective-permute-start.4) | collective-permute-done | bytes 501792 | tf_op jit(solution)/shard_map/ppermute | solution.py:39
  50.4 1.9 %bitcast_dynamic-update-slice_fusion.5 = bf16[8,112,2240]{2,1,0:T(8,128)(2,1)} fusion(bf16[8,112,2240]{2,1,0:T(8,128)(2,1)} %bitcast_dynamic-update-slice_fusion.6, bf16[112,2240]{1,0:T(8,128)(2,1)} %collective-permute-done.4), kind=kLoop, calls=%fused_computation.27 | loop fusion | bytes 1032192
  52.3 13.6 %collective-permute-done.5 = bf16[112,2240]{1,0:T(8,128)(2,1)S(1)} collective-permute-done((bf16[112,2240]{1,0:T(8,128)(2,1)}, bf16[112,2240]{1,0:T(8,128)(2,1)S(1)}, u32[]{:S(2)}, u32[]{:S(2)}) %collective-permute-start.5) | collective-permute-done | bytes 501792 | tf_op jit(solution)/shard_map/ppermute | solution.py:39
  65.9 0.8 %bitcast_dynamic-update-slice_fusion.4 = bf16[8,112,2240]{2,1,0:T(8,128)(2,1)} fusion(bf16[8,112,2240]{2,1,0:T(8,128)(2,1)} %bitcast_dynamic-update-slice_fusion.5, bf16[112,2240]{1,0:T(8,128)(2,1)S(1)} %collective-permute-done.5), kind=kLoop, calls=%fused_computation.26 | loop fusion | bytes 1017856
  66.7 0.8 %bitcast_dynamic-update-slice_fusion.3 = bf16[8,112,2240]{2,1,0:T(8,128)(2,1)} fusion(bf16[8,112,2240]{2,1,0:T(8,128)(2,1)} %bitcast_dynamic-update-slice_fusion.4, bf16[224,2240]{1,0:T(8,128)(2,1)S(1)} %copy-done.2, s32[]{:T(128)S(6)} %select_n.106), kind=kLoop, calls=%fused_computation.25 | loop fusion | bytes 1017860
  67.6 1.9 %bitcast_dynamic-update-slice_fusion.2 = bf16[8,112,2240]{2,1,0:T(8,128)(2,1)} fusion(bf16[8,112,2240]{2,1,0:T(8,128)(2,1)} %bitcast_dynamic-update-slice_fusion.3, bf16[112,2240]{1,0:T(8,128)(2,1)} %collective-permute-done.6), kind=kLoop, calls=%fused_computation.24 | loop fusion | bytes 1032192
  69.5 0.8 %bitcast_dynamic-update-slice_fusion.1 = bf16[8,112,2240]{2,1,0:T(8,128)(2,1)} fusion(bf16[8,112,2240]{2,1,0:T(8,128)(2,1)} %bitcast_dynamic-update-slice_fusion.2, bf16[112,2240]{1,0:T(8,128)(2,1)S(1)} %collective-permute-done.7), kind=kLoop, calls=%fused_computation.23 | loop fusion | bytes 1017856
  70.3 0.8 %bitcast_dynamic-update-slice_fusion = bf16[8,112,2240]{2,1,0:T(8,128)(2,1)} fusion(bf16[8,112,2240]{2,1,0:T(8,128)(2,1)} %bitcast_dynamic-update-slice_fusion.1, bf16[112,2240]{1,0:T(8,128)(2,1)S(1)} %collective-permute-done.8), kind=kLoop, calls=%fused_computation.22 | loop fusion | bytes 1017856 | tf_op jit(solution)/shard_map/stack | solution.py:42
  71.1 6.4 %fusion.2 = bf16[512,2240]{0,1:T(8,128)(2,1)} fusion(bf16[8,112,2240]{2,1,0:T(8,128)(2,1)} %bitcast_dynamic-update-slice_fusion, bf16[512,2240]{0,1:T(8,128)(2,1)S(1)} %copy-done.5, f32[2240]{0:T(1024)S(1)} %dynamic-slice_reduce_fusion, bf16[8,512,112]{1,2,0:T(8,128)(2,1)S(1)} %gather_fusion, pred[8]{0:T(512)(128)(4,1)S(1)} %copy-done.6), kind=kOutput, calls=%fused_computation.4 | convolution fusion | flops 2060255232 | bytes 9528072 | tf_op jit(solution)/shard_map/ktr,krc->tc/dot_general | solution.py:112
  (41 shorter events, 1.2 us)
Async XLA Ops:
  0.0 20.8 %copy-start = (f32[4,2240]{1,0:T(4,128)S(1)}, f32[4,2240]{1,0:T(4,128)}, u32[]{:S(2)}) copy-start(f32[4,2240]{1,0:T(4,128)} %param.11) | copy-start | bytes 107524
  0.0 17.3 %copy-start.1 = (bf16[224,2240]{1,0:T(8,128)(2,1)S(1)}, bf16[224,2240]{1,0:T(8,128)(2,1)}, u32[]{:S(2)}) copy-start(bf16[224,2240]{1,0:T(8,128)(2,1)} %param.10) | copy-start | bytes 3010564
  1.3 18.2 %copy-start.3 = (bf16[2048,224]{0,1:T(8,128)(2,1)S(1)}, bf16[2048,224]{0,1:T(8,128)(2,1)}, u32[]{:S(2)}) copy-start(bf16[2048,224]{0,1:T(8,128)(2,1)} %param.6) | copy-start | bytes 2752516
  3.0 15.3 %copy-start.4 = (pred[224,224]{1,0:T(8,128)(4,1)}, pred[224,224]{1,0:T(8,128)(4,1)S(1)}, u32[]{:S(2)}) copy-start(pred[224,224]{1,0:T(8,128)(4,1)S(1)} %broadcast_compare_fusion) | copy-start | bytes 150532
  5.8 15.9 %collective-permute-start.2 = (f32[2,113,112]{2,1,0:T(8,128)S(1)}, f32[2,113,112]{2,1,0:T(8,128)}, u32[]{:S(2)}, u32[]{:S(2)}) collective-permute-start(f32[2,113,112]{2,1,0:T(8,128)S(1)} %pad_maximum_fusion), channel_id=1, source_target_pairs={{0,12},{1,13},{2,14},{3,15},{16,28},{17,29},{18,30},{19,31}} | collective-permute-start | bytes 303752 | tf_op jit(solution)/shard_map/ppermute | solution.py:17
  13.4 8.2 %collective-permute-start = (f32[2,113,112]{2,1,0:T(8,128)S(1)}, f32[2,113,112]{2,1,0:T(8,128)}, u32[]{:S(2)}, u32[]{:S(2)}) collective-permute-start(f32[2,113,112]{2,1,0:T(8,128)S(1)} %pad_maximum_fusion), channel_id=1, source_target_pairs={{0,4},{4,8},{8,12},{1,5},{5,9},{9,13},{2,6},{6,10},{10,14},{3,7},{... | collective-permute-start | bytes 303752 | tf_op jit(solution)/shard_map/ppermute | solution.py:17
  15.3 6.3 %collective-permute-start.1 = (f32[2,113,112]{2,1,0:T(8,128)S(1)}, f32[2,113,112]{2,1,0:T(8,128)}, u32[]{:S(2)}, u32[]{:S(2)}) collective-permute-start(f32[2,113,112]{2,1,0:T(8,128)S(1)} %pad_maximum_fusion), channel_id=1, source_target_pairs={{0,8},{4,12},{1,9},{5,13},{2,10},{6,14},{3,11},{7,15},{16,24},{20,... | collective-permute-start | bytes 303752 | tf_op jit(solution)/shard_map/ppermute | solution.py:17
  18.3 15.2 %collective-permute-start.3 = (bf16[112,2240]{1,0:T(8,128)(2,1)}, bf16[112,2240]{1,0:T(8,128)(2,1)S(1)}, u32[]{:S(2)}, u32[]{:S(2)}) collective-permute-start(bf16[112,2240]{1,0:T(8,128)(2,1)} %get-tuple-element.6), channel_id=1, source_target_pairs={{0,4},{4,8},{8,12},{12,0},{1,5},{5,9},{9,13},{13,1},{2,6},{6,10},{... | collective-permute-start | bytes 1505288 | tf_op jit(solution)/shard_map/ppermute | solution.py:39
  28.2 38.5 %copy-start.2 = (bf16[224,2240]{1,0:T(8,128)(2,1)S(1)}, bf16[224,2240]{1,0:T(8,128)(2,1)}, u32[]{:S(2)}) copy-start(bf16[224,2240]{1,0:T(8,128)(2,1)} %param.10) | copy-start | bytes 3010564
  28.2 16.6 %all-to-all-start = ((bf16[4,512,224]{1,2,0:T(8,128)(2,1)}), bf16[4,512,224]{1,2,0:T(8,128)(2,1)S(1)}, u32[]{:S(2)}, u32[]{:S(2)}) async-start(bf16[4,512,224]{1,2,0:T(8,128)(2,1)} %divide_convert_fusion), calls=%async_computation | async-start | bytes 1835008 | tf_op jit(solution)/shard_map/all_to_all | solution.py:103
  33.5 16.9 %collective-permute-start.4 = (bf16[112,2240]{1,0:T(8,128)(2,1)S(1)}, bf16[112,2240]{1,0:T(8,128)(2,1)}, u32[]{:S(2)}, u32[]{:S(2)}) collective-permute-start(bf16[112,2240]{1,0:T(8,128)(2,1)S(1)} %collective-permute-done.3), channel_id=1, source_target_pairs={{0,4},{4,8},{8,12},{12,0},{1,5},{5,9},{9,13},{13,1},{2,6},{6,10},{... | collective-permute-start | bytes 1505288 | tf_op jit(solution)/shard_map/ppermute | solution.py:39
  35.2 32.3 %collective-permute-start.6 = (bf16[112,2240]{1,0:T(8,128)(2,1)S(1)}, bf16[112,2240]{1,0:T(8,128)(2,1)}, u32[]{:S(2)}, u32[]{:S(2)}) collective-permute-start(bf16[112,2240]{1,0:T(8,128)(2,1)S(1)} %collective-permute-done.3), channel_id=1, source_target_pairs={{0,1},{1,0},{2,3},{3,2},{4,5},{5,4},{6,7},{7,6},{8,9},{9,8},{10,11... | collective-permute-start | bytes 1505288 | tf_op jit(solution)/shard_map/ppermute | solution.py:41
  44.9 26.3 %copy-start.6 = (pred[8]{0:T(512)(128)(4,1)S(1)}, pred[8]{0:T(512)(128)(4,1)}, u32[]{:S(2)}) copy-start(pred[8]{0:T(512)(128)(4,1)} %compare_and_fusion) | copy-start | bytes 28
  45.7 25.4 %copy-start.5 = (bf16[512,2240]{0,1:T(8,128)(2,1)S(1)}, bf16[512,2240]{0,1:T(8,128)(2,1)}, u32[]{:S(2)}) copy-start(bf16[512,2240]{0,1:T(8,128)(2,1)} %param.9) | copy-start | bytes 6881284
  50.4 15.5 %collective-permute-start.5 = (bf16[112,2240]{1,0:T(8,128)(2,1)}, bf16[112,2240]{1,0:T(8,128)(2,1)S(1)}, u32[]{:S(2)}, u32[]{:S(2)}) collective-permute-start(bf16[112,2240]{1,0:T(8,128)(2,1)} %collective-permute-done.4), channel_id=1, source_target_pairs={{0,4},{4,8},{8,12},{12,0},{1,5},{5,9},{9,13},{13,1},{2,6},{6,10},{... | collective-permute-start | bytes 1505288 | tf_op jit(solution)/shard_map/ppermute | solution.py:39
  50.4 19.1 %collective-permute-start.7 = (bf16[112,2240]{1,0:T(8,128)(2,1)}, bf16[112,2240]{1,0:T(8,128)(2,1)S(1)}, u32[]{:S(2)}, u32[]{:S(2)}) collective-permute-start(bf16[112,2240]{1,0:T(8,128)(2,1)} %collective-permute-done.4), channel_id=1, source_target_pairs={{0,1},{1,0},{2,3},{3,2},{4,5},{5,4},{6,7},{7,6},{8,9},{9,8},{10,11... | collective-permute-start | bytes 1505288 | tf_op jit(solution)/shard_map/ppermute | solution.py:41
  65.9 4.4 %collective-permute-start.8 = (bf16[112,2240]{1,0:T(8,128)(2,1)S(1)}, bf16[112,2240]{1,0:T(8,128)(2,1)S(1)}, u32[]{:S(2)}, u32[]{:S(2)}) collective-permute-start(bf16[112,2240]{1,0:T(8,128)(2,1)S(1)} %collective-permute-done.5), channel_id=1, source_target_pairs={{0,1},{1,0},{2,3},{3,2},{4,5},{5,4},{6,7},{7,6},{8,9},{9,8},{10,11... | collective-permute-start | bytes 1505288 | tf_op jit(solution)/shard_map/ppermute | solution.py:41
